TPU v7x, 32 devices: a whole 2x2x4 slice. The times are simulated.
32 devices in a mesh: req: 8 (over z, y), tp: 4 (over x, core).
Axes of the slice: x: 2, y: 2, z: 4, core: 2. Of those that a mesh axis runs over, the one named last changes fastest.
Arguments:
- hidden: bfloat16 [4096, 2048], P('req', 'tp'), may hold values from -6 to 6
- queries: bfloat16 [4096, 2048], P('req', 'tp'), may hold values from -4 to 4
- new_keys: bfloat16 [4096, 512], P('req'), may hold values from -4 to 4
- new_values: bfloat16 [4096, 512], P('req'), may hold values from -6 to 6
- cache_keys: bfloat16 [384, 64, 512], P('req'), may hold values from -6 to 6
- cache_values: bfloat16 [384, 64, 512], P('req'), may hold values from -6 to 6
- out_weight: bfloat16 [2048, 2048], P('tp'), may hold values from -0.125 to 0.125
- attn_gain: bfloat16 [2048], P('tp'), may hold values from 0.099609375 to 1.8984375
- ple_input: bfloat16 [4096, 256], P('req'), may hold values from -6 to 6
- ple_gate_weight: bfloat16 [2048, 256], P('tp'), may hold values from -0.125 to 0.125
- ple_proj_weight: bfloat16 [256, 2048], P(None, 'tp'), may hold values from -0.375 to 0.375
- ple_gain: bfloat16 [2048], P('tp'), may hold values from 0.099609375 to 1.8984375
- page_holder: int32 [384, 1], P('req'), may hold values from 0 to 7; in each aligned block of 48 rows (0 to 47, 48 to 95, ...) at most 6 rows name the same one
- page_slot: int32 [384, 1], P('req'), may hold values from 0 to 47
- page_counts: int32 [8, 8], P('req'), may hold values from 1 to 12, 48 in all within a row
- last_fill: int32 [8, 8], P('req'), may hold values from 1 to 64
- row_counts: int32 [8, 8], P('req'), may hold values from 1 to 256, 512 in all within a row
Outputs:
- layer_out: bfloat16 [4096, 2048], P('req', 'tp')
Inputs may be any that keep to these rules, and one draw needn't show every extreme that they name: `page_holder`: within the 48 page references of one device's requests (aligned blocks), no req index is named more than 6 times; in some block one is named exactly 6 times. `page_counts`: the 8 counts of one device sum to 48; some count equals 12. `row_counts`: the 8 counts of one device sum to 512; some count equals 256.
All inputs are finite; a program needn't handle non-finite values.
Results may differ from a plain program's by a relative error of at most 0.0061.
Values may be sent and summed in bfloat16 or wider, within the bound.
No kernel may reach another device: no remote copies, remote signals or barrier semaphores. Data moves between devices by JAX's collectives and lax.ppermute only.
A program may use at most 128 MiB of HBM per device.

v0:
```python
import math
import jax
import jax.numpy as jnp
from jax import lax
from jax.sharding import PartitionSpec as P

D = 2048
HD = 256


def slot_lookup(positions, counts):
    starts = jnp.cumsum(counts) - counts
    owning = jnp.sum((positions[:, None] >= starts[None, :]).astype(jnp.int32), axis=1) - 1
    return (owning, starts)


def table_pick(table, owning):
    onehot = owning[:, None] == jnp.arange(table.shape[0], dtype=jnp.int32)[None, :]
    return jnp.sum(jnp.where(onehot, table[None, :], 0), axis=1)


def attend_masks(counts_of_pages, fill_row, counts_of_rows, page_len, page_total, row_total):
    key_index = jnp.arange(page_total * page_len, dtype=jnp.int32)
    page_ref = key_index // page_len
    within = key_index % page_len
    page_owner, page_starts = slot_lookup(page_ref, counts_of_pages)
    context_len = (counts_of_pages - 1) * page_len + fill_row
    position = (page_ref - table_pick(page_starts, page_owner)) * page_len + within
    valid = position < table_pick(context_len, page_owner)
    row_index = jnp.arange(row_total, dtype=jnp.int32)
    row_owner = slot_lookup(row_index, counts_of_rows)[0]
    context_mask = (row_owner[:, None] == page_owner[None, :]) & valid[None, :]
    causal = (row_owner[:, None] == row_owner[None, :]) & (row_index[None, :] <= row_index[:, None])
    return jnp.concatenate([context_mask, causal], axis=1)


def shards(
    hidden,
    queries,
    new_keys,
    new_values,
    cache_keys,
    cache_values,
    out_weight,
    attn_gain,
    ple_input,
    ple_gate_weight,
    ple_proj_weight,
    ple_gain,
    page_holder,
    page_slot,
    page_counts,
    last_fill,
    row_counts,
):
    row_total = hidden.shape[0]
    page_total = cache_keys.shape[0]
    page_len = cache_keys.shape[1]
    req_count = lax.axis_size("req")
    tp_index = lax.axis_index("tp")
    local_heads = queries.shape[1] // HD
    kv_head = tp_index // 2
    capacity = max(2, page_total // req_count)
    holders = page_holder[:, 0]
    places = page_slot[:, 0]
    ref_index = jnp.arange(page_total, dtype=jnp.int32)
    earlier = (holders[:, None] == holders[None, :]) & (ref_index[:, None] > ref_index[None, :])
    ranking = jnp.sum(earlier.astype(jnp.int32), axis=1)
    matched = (holders[:, None, None] == jnp.arange(req_count, dtype=jnp.int32)[None, :, None]) & (
        ranking[:, None, None] == jnp.arange(capacity, dtype=jnp.int32)[None, None, :]
    )
    request_table = jnp.sum(jnp.where(matched, places[:, None, None] + 1, 0), axis=0) - 1
    asked = lax.all_to_all(request_table, "req", split_axis=0, concat_axis=0, tiled=True)
    wanted = jnp.maximum(asked, 0)
    head_keys = lax.dynamic_slice_in_dim(cache_keys, kv_head * HD, HD, 2)
    head_values = lax.dynamic_slice_in_dim(cache_values, kv_head * HD, HD, 2)
    stacked = jnp.concatenate([head_keys, head_values], axis=2)
    arrival_index = holders * capacity + ranking
    outgoing = stacked[wanted]
    arrived = lax.all_to_all(outgoing, "req", split_axis=0, concat_axis=0, tiled=True)
    context = arrived.reshape(req_count * capacity, page_len, 2 * HD)[arrival_index]
    context_keys = context[:, :, :HD].reshape(page_total * page_len, HD)
    context_values = context[:, :, HD:].reshape(page_total * page_len, HD)
    fresh_keys = lax.dynamic_slice_in_dim(new_keys, kv_head * HD, HD, 1)
    fresh_values = lax.dynamic_slice_in_dim(new_values, kv_head * HD, HD, 1)
    all_keys = jnp.concatenate([context_keys, fresh_keys], axis=0)
    all_values = jnp.concatenate([context_values, fresh_values], axis=0)
    masking = attend_masks(
        page_counts[0], last_fill[0], row_counts[0], page_len, page_total, row_total
    )
    query_rows = queries.reshape(row_total, local_heads, HD)
    scores = jnp.einsum("rhd,kd->hrk", query_rows, all_keys, preferred_element_type=jnp.float32) * (
        1.0 / math.sqrt(HD)
    )
    scores = jnp.where(masking[None], scores, -1e30)
    highest = jnp.max(scores, axis=-1, keepdims=True)
    expo = jnp.exp(scores - highest)
    weights = (expo / jnp.sum(expo, axis=-1, keepdims=True)).astype(jnp.bfloat16)
    attention = jnp.einsum("hrk,kd->rhd", weights, all_values, preferred_element_type=jnp.float32)
    attention = attention.astype(jnp.bfloat16).reshape(row_total, local_heads * HD)
    tp_size = lax.axis_size("tp")
    full_weight = lax.all_gather(out_weight, "tp", axis=0, tiled=True)
    full_gate_weight = lax.all_gather(ple_gate_weight, "tp", axis=0, tiled=True)
    full_proj_weight = lax.all_gather(ple_proj_weight, "tp", axis=1, tiled=True)
    full_attn_gain = lax.all_gather(attn_gain, "tp", axis=0, tiled=True)
    full_ple_gain = lax.all_gather(ple_gain, "tp", axis=0, tiled=True)
    row_hidden = lax.all_to_all(hidden, "tp", split_axis=0, concat_axis=1, tiled=True)
    row_attention = lax.all_to_all(attention, "tp", split_axis=0, concat_axis=1, tiled=True)
    part_rows = row_attention.shape[0]
    row_ple = lax.dynamic_slice_in_dim(ple_input, tp_index * part_rows, part_rows, 0)
    projected = jnp.dot(row_attention, full_weight, preferred_element_type=jnp.float32)
    squares = jnp.sum(projected * projected, axis=1)
    normed = (
        projected
        * lax.rsqrt(squares / D + 1e-06)[:, None]
        * full_attn_gain.astype(jnp.float32)[None, :]
    )
    mixed_state = (row_hidden.astype(jnp.float32) + normed).astype(jnp.bfloat16)
    gate = jnp.dot(mixed_state, full_gate_weight, preferred_element_type=jnp.float32)
    activated = (jax.nn.gelu(gate, approximate=True) * row_ple.astype(jnp.float32)).astype(
        jnp.bfloat16
    )
    lifted = jnp.dot(activated, full_proj_weight, preferred_element_type=jnp.float32)
    lift_squares = jnp.sum(lifted * lifted, axis=1)
    lift_normed = (
        lifted
        * lax.rsqrt(lift_squares / D + 1e-06)[:, None]
        * full_ple_gain.astype(jnp.float32)[None, :]
    )
    row_out = (mixed_state.astype(jnp.float32) + lift_normed).astype(jnp.bfloat16)
    return lax.all_to_all(row_out, "tp", split_axis=1, concat_axis=0, tiled=True)


def solution(mesh):
    return jax.shard_map(
        shards,
        mesh=mesh,
        in_specs=(
            P("req", "tp"),
            P("req", "tp"),
            P("req", None),
            P("req", None),
            P("req", None, None),
            P("req", None, None),
            P("tp", None),
            P("tp"),
            P("req", None),
            P("tp", None),
            P(None, "tp"),
            P("tp"),
            P("req", None),
            P("req", None),
            P("req", None),
            P("req", None),
            P("req", None),
        ),
        out_specs=P("req", "tp"),
        check_vma=False,
    )
```

profile of v0, /device:TPU:0, one launch (start us, length us, event | category | flops | bytes accessed | tf_op | source)
XLA Modules:
  0.0 189.8 jit_solution(16006355638064620231)
XLA Ops:
  6.5 0.7 all-gather.6.cloned.1.call-update
  7.3 0.9 convert_reduce_fusion.1
  8.2 0.7 add_bitcast_fusion.2
  9.7 0.7 copy.41
  10.4 7.3 %all-to-all-start.1 = ((s32[8,1,6]{2,1,0:T(1,128)}), s32[8,1,6]{2,1,0:T(1,128)S(1)}, u32[]{:S(2)}, u32[]{:S(2)}) async-start(s32[8,1,6]{2,1,0:T(1,128)} %copy.41), calls=%async_computation.1 | async-start | bytes 8192 | tf_op jit(solution)/shard_map/all_to_all | solution.py:73
  17.7 2.7 %constant_dynamic-slice_fusion.2 = (bf16[48,64,256]{2,1,0:T(8,128)(2,1)S(1)}, bf16[48,64,256]{2,1,0:T(8,128)(2,1)S(1)}) fusion(bf16[48,64,512]{2,1,0:T(8,128)(2,1)} %param.22, s32[]{:T(128)S(6)} %select_n.60, bf16[48,64,512]{2,1,0:T(8,128)(2,1)} %param.21), kind=kLoop, calls=%fused_computation.83 | loop fusion | bytes 6291460 | tf_op jit(solution)/shard_map/dynamic_slice | solution.py:76
  20.6 3.4 %all-to-all-done.1 = s32[8,1,6]{2,1,0:T(1,128)S(1)} async-done(((s32[8,1,6]{2,1,0:T(1,128)}), s32[8,1,6]{2,1,0:T(1,128)S(1)}, u32[]{:S(2)}, u32[]{:S(2)}) %all-to-all-start.1) | async-done | bytes 224 | tf_op jit(solution)/shard_map/all_to_all | solution.py:73
  24.2 2.5 %gather_fusion = bf16[48,64,512]{2,1,0:T(8,128)(2,1)} fusion(bf16[48,64,512]{2,1,0:T(8,128)(2,1)S(1)} %pad_maximum_fusion, s32[1024]{0:T(1024)S(1)} %pad_clamp_fusion.1), kind=kCustom, calls=%fused_computation | custom fusion | bytes 6291648 | tf_op jit(solution)/shard_map/gather | solution.py:79
  26.7 3.8 %all-to-all-start.2 = ((bf16[8,6,64,512]{3,2,1,0:T(8,128)(2,1)}), bf16[8,6,64,512]{3,2,1,0:T(8,128)(2,1)S(1)}, u32[]{:S(2)}, u32[]{:S(2)}) async-start(bf16[8,6,64,512]{3,2,1,0:T(8,128)(2,1)} %bitcast.73), calls=%async_computation.2 | async-start | bytes 6291456 | tf_op jit(solution)/shard_map/all_to_all | solution.py:80
  30.5 0.7 all-gather.10.cloned.1.call-update
  31.6 1.8 constant_dynamic-slice_fusion
  33.4 0.8 copy.51
  34.8 2.4 %compare_and_fusion = pred[512,3072]{0,1:T(8,128)(4,1)S(1)} fusion(s32[512]{0:T(512)S(1)} %broadcast_add_fusion.1, s32[3072]{0:T(1024)S(1)} %broadcast_add_fusion, pred[3072]{0:T(1024)(128)(4,1)S(1)} %fusion.40), kind=kLoop, calls=%fused_computation.12 | loop fusion | flops 3145728 | bytes 1590272 | tf_op jit(solution)/shard_map/and | solution.py:32
  37.2 1.7 pad_add_fusion
  38.9 61.1 %all-to-all-done.2 = bf16[8,6,64,512]{3,2,1,0:T(8,128)(2,1)S(1)} async-done(((bf16[8,6,64,512]{3,2,1,0:T(8,128)(2,1)}), bf16[8,6,64,512]{3,2,1,0:T(8,128)(2,1)S(1)}, u32[]{:S(2)}, u32[]{:S(2)}) %all-to-all-start.2) | async-done | bytes 3145760 | tf_op jit(solution)/shard_map/all_to_all | solution.py:80
  100.0 4.1 %all-to-all-start = ((bf16[4,128,512]{2,1,0:T(8,128)(2,1)}), bf16[4,128,512]{2,1,0:T(8,128)(2,1)}, u32[]{:S(2)}, u32[]{:S(2)}) async-start(bf16[4,128,512]{2,1,0:T(8,128)(2,1)} %bitcast.82), calls=%async_computation | async-start | bytes 1048576 | tf_op jit(solution)/shard_map/all_to_all | solution.py:107
  104.1 2.5 %gather_fusion.1 = bf16[48,64,512]{2,1,0:T(8,128)(2,1)} fusion(bf16[48,64,512]{2,1,0:T(8,128)(2,1)S(1)} %bitcast.72, s32[1024]{0:T(1024)S(1)} %pad_clamp_fusion), kind=kCustom, calls=%fused_computation.1 | custom fusion | bytes 6291648 | tf_op jit(solution)/shard_map/gather | solution.py:81
  106.6 2.1 %fusion.52 = (bf16[48,64,256]{2,1,0:T(8,128)(2,1)S(1)}, bf16[48,64,256]{2,1,0:T(8,128)(2,1)S(1)}) fusion(bf16[48,64,512]{2,1,0:T(8,128)(2,1)} %gather_fusion.1), kind=kLoop, calls=%fused_computation.102 | loop fusion | bytes 6291456 | tf_op jit(solution)/shard_map/slice | solution.py:83
  108.7 1.8 copy.43
  110.5 8.6 %fusion.8 = f32[3584,512,2]{1,0,2:T(8,128)} fusion(bf16[512,256]{1,0:T(8,128)(2,1)} %get-tuple-element.17, bf16[3072,256]{1,0:T(8,128)(2,1)S(1)} %bitcast.74, bf16[64,2,8,256]{3,2,1,0:T(8,128)(2,1)} %bitcast.81), kind=kOutput, calls=%fused_computation.18 | convolution fusion | flops 1882718208 | bytes 17039360 | tf_op jit(solution)/shard_map/rhd,kd->hrk/dot_general | solution.py:92
  119.1 16.0 %fusion.53 = (f32[2,512]{1,0:T(2,128)S(1)}, f32[2,512,3584]{1,2,0:T(8,128)}) fusion(f32[3584,512,2]{1,0,2:T(8,128)} %fusion.8, pred[512,3584]{0,1:T(8,128)(4,1)S(1)} %copy-done), kind=kOutput, calls=%fused_computation.103 | output fusion | flops 22023680 | bytes 31199232 | tf_op jit(solution)/shard_map/sub | solution.py:97
  135.0 7.3 %fusion.12 = bf16[512,2,256]{0,2,1:T(8,128)(2,1)S(1)} fusion(f32[2,512,3584]{1,2,0:T(8,128)} %get-tuple-element.12, f32[2,512]{1,0:T(2,128)S(1)} %get-tuple-element.11, bf16[512,256]{0,1:T(8,128)(2,1)} %copy.51, bf16[3072,256]{0,1:T(8,128)(2,1)S(1)} %copy-done.1), kind=kOutput, calls=%fused_computation.22 | convolution fusion | flops 1890320384 | bytes 17043456 | tf_op jit(solution)/shard_map/hrk,kd->rhd/dot_general | solution.py:99
  142.5 0.9 copy.46
  143.4 3.7 %all-to-all-start.3 = ((bf16[4,128,512]{1,2,0:T(8,128)(2,1)}), bf16[4,128,512]{1,2,0:T(8,128)(2,1)S(1)}, u32[]{:S(2)}, u32[]{:S(2)}) async-start(bf16[4,128,512]{1,2,0:T(8,128)(2,1)} %copy.46), calls=%async_computation.3 | async-start | bytes 1048576 | tf_op jit(solution)/shard_map/all_to_all | solution.py:108
  147.1 0.7 all-gather.8.cloned.1.call-update
  147.8 9.0 %all-gather = bf16[4,1,512]{2,1,0:T(2,128)(2,1)S(1)} all-gather(bf16[1,1,512]{2,1,0:T(2,128)(2,1)S(1)} %reshape.210), channel_id=1, replica_groups=mesh['req'=8,'tp'=4] {'tp'}, dimensions={0}, use_global_device_ids=true | all-gather | bytes 5120 | tf_op jit(solution)/shard_map/all_gather | solution.py:105
  156.8 5.2 %all-gather.1 = bf16[4,1,512]{2,1,0:T(2,128)(2,1)S(1)} all-gather(bf16[1,1,512]{2,1,0:T(2,128)(2,1)S(1)} %reshape.212), channel_id=1, replica_groups=mesh['req'=8,'tp'=4] {'tp'}, dimensions={0}, use_global_device_ids=true | all-gather | bytes 5120 | tf_op jit(solution)/shard_map/all_gather | solution.py:106
  162.0 1.2 convert_bitcast_fusion
  163.4 4.8 %multiply_reduce_fusion.1 = (f32[128]{0:T(128)S(1)}, f32[128,2048]{1,0:T(8,128)S(1)}) fusion(bf16[128,2048]{0,1:T(8,128)(2,1)S(1)} %bitcast.77, bf16[2048,2048]{1,0:T(8,128)(2,1)} %all-gather.6.cloned.1.call-done), kind=kOutput, calls=%fused_computation.27 | convolution fusion | flops 1074265984 | bytes 9961984 | tf_op jit(solution)/shard_map/dot_general | solution.py:111
  168.4 2.5 %multiply_reduce_fusion = (f32[128]{0:T(128)S(1)}, f32[128,2048]{1,0:T(8,128)S(1)}) fusion(bf16[256,2048]{1,0:T(8,128)(2,1)} %all-gather.10.cloned.1.call-done, bf16[512,256]{1,0:T(8,128)(2,1)} %param.25, s32[]{:T(128)S(6)} %select_n.68, bf16[128,2048]{1,0:T(8,128)(2,1)S(1)} %add_convert_fusion.1, bf16[2048,256]{1,0:T(8,128)(2,1)} %all-gather.8.cloned.1.call-done), kind=kOutput, calls=%fused_computation.25 | convolution fusion | flops 269320064 | bytes 3736068 | tf_op jit(solution)/shard_map/dot_general | solution.py:123
  171.2 11.2 %all_to_all.62 = bf16[128,4,512]{2,0,1:T(8,128)(2,1)S(1)} all-to-all(bf16[128,4,512]{2,0,1:T(8,128)(2,1)S(1)} %bitcast.79), channel_id=1, replica_groups=mesh['req'=8,'tp'=4] {'tp'}, dimensions={1} | all-to-all | bytes 1048576 | tf_op jit(solution)/shard_map/all_to_all | solution.py:131
  182.4 0.8 copy.62
  (57 shorter events, 3.1 us)
Async XLA Ops:
  6.5 156.8 %all-gather.6.cloned.1.call-start = ((), (), s32[]{:S(2)}) async-start(), calls=%async_computation.5 | async-start | bytes 10485760 | tf_op jit(solution)/shard_map/all_gather | solution.py:102
  10.4 13.7 %all-to-all-start.1 = ((s32[8,1,6]{2,1,0:T(1,128)}), s32[8,1,6]{2,1,0:T(1,128)S(1)}, u32[]{:S(2)}, u32[]{:S(2)}) async-start(s32[8,1,6]{2,1,0:T(1,128)} %copy.41), calls=%async_computation.1 | async-start | bytes 8192 | tf_op jit(solution)/shard_map/all_to_all | solution.py:73
  26.7 4.6 %copy-start.5 = (s32[1,8]{1,0:T(1,128)S(1)}, s32[1,8]{1,0:T(1,128)}, u32[]{:S(2)}) copy-start(s32[1,8]{1,0:T(1,128)} %param.31) | copy-start | bytes 100
  26.7 4.8 %copy-start.7 = (s32[1,8]{1,0:T(1,128)S(1)}, s32[1,8]{1,0:T(1,128)}, u32[]{:S(2)}) copy-start(s32[1,8]{1,0:T(1,128)} %param.33) | copy-start | bytes 100
  26.7 7.5 %copy-start.6 = (s32[48,1]{0,1:T(1,128)S(1)}, s32[48,1]{0,1:T(1,128)}, u32[]{:S(2)}) copy-start(s32[48,1]{0,1:T(1,128)} %param.29) | copy-start | bytes 580
  26.7 7.7 %copy-start.4 = (s32[1,8]{1,0:T(1,128)S(1)}, s32[1,8]{1,0:T(1,128)}, u32[]{:S(2)}) copy-start(s32[1,8]{1,0:T(1,128)} %param.32) | copy-start | bytes 100
  26.7 73.3 %all-to-all-start.2 = ((bf16[8,6,64,512]{3,2,1,0:T(8,128)(2,1)}), bf16[8,6,64,512]{3,2,1,0:T(8,128)(2,1)S(1)}, u32[]{:S(2)}, u32[]{:S(2)}) async-start(bf16[8,6,64,512]{3,2,1,0:T(8,128)(2,1)} %bitcast.73), calls=%async_computation.2 | async-start | bytes 6291456 | tf_op jit(solution)/shard_map/all_to_all | solution.py:80
  30.5 137.9 %all-gather.10.cloned.1.call-start = ((), (), s32[]{:S(2)}) async-start(), calls=%async_computation.7 | async-start | bytes 1310720 | tf_op jit(solution)/shard_map/all_gather | solution.py:104
  100.0 43.4 %all-to-all-start = ((bf16[4,128,512]{2,1,0:T(8,128)(2,1)}), bf16[4,128,512]{2,1,0:T(8,128)(2,1)}, u32[]{:S(2)}, u32[]{:S(2)}) async-start(bf16[4,128,512]{2,1,0:T(8,128)(2,1)} %bitcast.82), calls=%async_computation | async-start | bytes 1048576 | tf_op jit(solution)/shard_map/all_to_all | solution.py:107
  110.5 8.6 %copy-start = (pred[512,3584]{0,1:T(8,128)(4,1)S(1)}, pred[512,3584]{0,1:T(8,128)(4,1)}, u32[]{:S(2)}) copy-start(pred[512,3584]{0,1:T(8,128)(4,1)} %pad_add_fusion) | copy-start | bytes 5505028
  119.1 16.0 %copy-start.1 = (bf16[3072,256]{0,1:T(8,128)(2,1)S(1)}, bf16[3072,256]{0,1:T(8,128)(2,1)}, u32[]{:S(2)}) copy-start(bf16[3072,256]{0,1:T(8,128)(2,1)} %copy.43) | copy-start | bytes 4718596
  142.4 5.4 %copy-start.2 = (bf16[512]{0:T(512)(128)(2,1)S(1)}, bf16[512]{0:T(512)(128)(2,1)}, u32[]{:S(2)}) copy-start(bf16[512]{0:T(512)(128)(2,1)} %param.24) | copy-start | bytes 3076
  142.4 14.4 %copy-start.3 = (bf16[512]{0:T(512)(128)(2,1)S(1)}, bf16[512]{0:T(512)(128)(2,1)}, u32[]{:S(2)}) copy-start(bf16[512]{0:T(512)(128)(2,1)} %param.28) | copy-start | bytes 3076
  143.4 19.9 %all-to-all-start.3 = ((bf16[4,128,512]{1,2,0:T(8,128)(2,1)}), bf16[4,128,512]{1,2,0:T(8,128)(2,1)S(1)}, u32[]{:S(2)}, u32[]{:S(2)}) async-start(bf16[4,128,512]{1,2,0:T(8,128)(2,1)} %copy.46), calls=%async_computation.3 | async-start | bytes 1048576 | tf_op jit(solution)/shard_map/all_to_all | solution.py:108
  147.1 21.4 %all-gather.8.cloned.1.call-start = ((), (), s32[]{:S(2)}) async-start(), calls=%async_computation.6 | async-start | bytes 1310720 | tf_op jit(solution)/shard_map/all_gather | solution.py:103
Sparse Core Ops, SparseCore 0:
  8.9 60.9 all-gather.5
  71.5 16.7 all-gather.9
  149.5 16.2 all-gather.7
where the time goes:
time: 190 us
  waiting for transfers between devices  66.7 us (35%)
  blocking collectives  25.4 us (13%)
  other arithmetic  25.3 us (13%)
  matrix products  23.1 us (12%)
  starting transfers between devices  19 us (10%)
  local copies, waits for them, and re-layouts  16.9 us (9%)
  between operations  13.4 us (7%)
    all_to_all x1, waiting for transfers between devices, shards(): lax.all_to_all(outgoing, 'req', split_axis=0, concat_axis=0, tiled=True)  61.1 us
    sub x1, other arithmetic, shards(): expo = jnp.exp(scores - highest)  16 us
    all_to_all x1, blocking collectives, shards(): lax.all_to_all(row_out, 'tp', split_axis=1, concat_axis=0, tiled=True)  11.2 us
    all_gather x1, blocking collectives, shards(): full_attn_gain = lax.all_gather(attn_gain, 'tp', axis=0, tiled=True)  8.99 us
    dot_general x1, matrix products, shards(): jnp.einsum('rhd,kd->hrk', query_rows, all_keys, preferred_element_type=jn...  8.55 us
    dot_general x1, matrix products, shards(): jnp.einsum('hrk,kd->rhd', weights, all_values, preferred_element_type=jnp...  7.33 us
    all_to_all x1, starting transfers between devices, shards(): lax.all_to_all(request_table, 'req', split_axis=0, concat_axis=0, tiled=T...  7.28 us
    all_gather x1, blocking collectives, shards(): full_ple_gain = lax.all_gather(ple_gain, 'tp', axis=0, tiled=True)  5.18 us
  transfers between devices with their start and end apart: 7, of which 2 were waited for; matrix products, arithmetic and copies ran while one was open for 32% of the time, Pallas kernels for 0%

commit v1 on v0

--- a/solution.py
+++ b/solution.py
@@ -104,7 +104,10 @@
     full_proj_weight = lax.all_gather(ple_proj_weight, "tp", axis=1, tiled=True)
     full_attn_gain = lax.all_gather(attn_gain, "tp", axis=0, tiled=True)
     full_ple_gain = lax.all_gather(ple_gain, "tp", axis=0, tiled=True)
-    row_hidden = lax.all_to_all(hidden, "tp", split_axis=0, concat_axis=1, tiled=True)
+    row_hidden = jnp.concatenate(
+        lax.all_to_all(jnp.stack(jnp.split(hidden, lax.axis_size("tp"), axis=0)), "tp", 0, 0),
+        axis=1,
+    )
     row_attention = lax.all_to_all(attention, "tp", split_axis=0, concat_axis=1, tiled=True)
     part_rows = row_attention.shape[0]
     row_ple = lax.dynamic_slice_in_dim(ple_input, tp_index * part_rows, part_rows, 0)

time: 190 us -> 190 us (level)
  waiting for transfers between devices: 66.7 us -> 64.7 us
    all_to_all x1, waiting for transfers between devices: 61.1 us -> 59.1 us  [shards(): lax.all_to_all(outgoing, 'req', split_axis=0, concat_axis=0, tiled=True)]
  transfers between devices with their start and end apart: 7 -> 7, of which waited for: 2 -> 2; matrix products, arithmetic and copies ran while one was open for 32% -> 34% of each run, Pallas kernels for 0% -> 0%
where the time goes in v1:
time: 190 us
  waiting for transfers between devices  64.7 us (34%)
  other arithmetic  26.2 us (14%)
  blocking collectives  25.4 us (13%)
  matrix products  23.2 us (12%)
  starting transfers between devices  18.9 us (10%)
  local copies, waits for them, and re-layouts  18 us (9%)
  between operations  13.4 us (7%)
    all_to_all x1, waiting for transfers between devices, shards(): lax.all_to_all(outgoing, 'req', split_axis=0, concat_axis=0, tiled=True)  59.1 us
    sub x1, other arithmetic, shards(): expo = jnp.exp(scores - highest)  16 us
    all_to_all x1, blocking collectives, shards(): lax.all_to_all(row_out, 'tp', split_axis=1, concat_axis=0, tiled=True)  11.2 us
    all_gather x1, blocking collectives, shards(): full_attn_gain = lax.all_gather(attn_gain, 'tp', axis=0, tiled=True)  8.99 us
    dot_general x1, matrix products, shards(): jnp.einsum('rhd,kd->hrk', query_rows, all_keys, preferred_element_type=jn...  8.58 us
    dot_general x1, matrix products, shards(): jnp.einsum('hrk,kd->rhd', weights, all_values, preferred_element_type=jnp...  7.33 us
    all_to_all x1, starting transfers between devices, shards(): lax.all_to_all(request_table, 'req', split_axis=0, concat_axis=0, tiled=T...  7.28 us
    all_gather x1, blocking collectives, shards(): full_ple_gain = lax.all_gather(ple_gain, 'tp', axis=0, tiled=True)  5.18 us
  transfers between devices with their start and end apart: 7, of which 2 were waited for; matrix products, arithmetic and copies ran while one was open for 34% of the time, Pallas kernels for 0%

profile of v1, /device:TPU:0, one launch (start us, length us, event | category | flops | bytes accessed | tf_op | source)
XLA Modules:
  0.0 189.8 jit_solution(9078734703025695744)
XLA Ops:
  6.5 0.7 all-gather.6.cloned.1.call-update
  7.3 0.9 convert_reduce_fusion.1
  10.4 7.3 %all-to-all-start.1 = ((s32[8,1,6]{2,1,0:T(1,128)}), s32[8,1,6]{2,1,0:T(1,128)S(1)}, u32[]{:S(2)}, u32[]{:S(2)}) async-start(s32[8,1,6]{2,1,0:T(1,128)} %copy.41), calls=%async_computation.1 | async-start | bytes 8192 | tf_op jit(solution)/shard_map/all_to_all | solution.py:73
  17.7 2.7 %constant_dynamic-slice_fusion.2 = (bf16[48,64,256]{2,1,0:T(8,128)(2,1)S(1)}, bf16[48,64,256]{2,1,0:T(8,128)(2,1)S(1)}) fusion(bf16[48,64,512]{2,1,0:T(8,128)(2,1)} %param.22, s32[]{:T(128)S(6)} %select_n.60, bf16[48,64,512]{2,1,0:T(8,128)(2,1)} %param.21), kind=kLoop, calls=%fused_computation.88 | loop fusion | bytes 6291460 | tf_op jit(solution)/shard_map/dynamic_slice | solution.py:76
  20.6 3.4 %all-to-all-done.1 = s32[8,1,6]{2,1,0:T(1,128)S(1)} async-done(((s32[8,1,6]{2,1,0:T(1,128)}), s32[8,1,6]{2,1,0:T(1,128)S(1)}, u32[]{:S(2)}, u32[]{:S(2)}) %all-to-all-start.1) | async-done | bytes 224 | tf_op jit(solution)/shard_map/all_to_all | solution.py:73
  24.2 2.5 %gather_fusion = bf16[48,64,512]{2,1,0:T(8,128)(2,1)} fusion(bf16[48,64,512]{2,1,0:T(8,128)(2,1)S(1)} %pad_maximum_fusion, s32[1024]{0:T(1024)S(1)} %pad_clamp_fusion.1), kind=kCustom, calls=%fused_computation | custom fusion | bytes 6291648 | tf_op jit(solution)/shard_map/gather | solution.py:79
  26.7 3.8 %all-to-all-start.2 = ((bf16[8,6,64,512]{3,2,1,0:T(8,128)(2,1)}), bf16[8,6,64,512]{3,2,1,0:T(8,128)(2,1)S(1)}, u32[]{:S(2)}, u32[]{:S(2)}) async-start(bf16[8,6,64,512]{3,2,1,0:T(8,128)(2,1)} %bitcast.80), calls=%async_computation.2 | async-start | bytes 6291456 | tf_op jit(solution)/shard_map/all_to_all | solution.py:80
  30.5 0.7 all-gather.10.cloned.1.call-update
  31.6 1.8 constant_dynamic-slice_fusion
  33.4 0.8 copy.51
  34.6 1.1 slice_bitcast_fusion.3
  35.7 0.9 pad_maximum_fusion.1
  36.8 2.4 %compare_and_fusion = pred[512,3072]{0,1:T(8,128)(4,1)S(1)} fusion(s32[512]{0:T(512)S(1)} %broadcast_add_fusion.1, s32[3072]{0:T(1024)S(1)} %broadcast_add_fusion, pred[3072]{0:T(1024)(128)(4,1)S(1)} %fusion.40), kind=kLoop, calls=%fused_computation.12 | loop fusion | flops 3145728 | bytes 1590272 | tf_op jit(solution)/shard_map/and | solution.py:32
  39.2 1.6 pad_add_fusion
  40.8 59.1 %all-to-all-done.2 = bf16[8,6,64,512]{3,2,1,0:T(8,128)(2,1)S(1)} async-done(((bf16[8,6,64,512]{3,2,1,0:T(8,128)(2,1)}), bf16[8,6,64,512]{3,2,1,0:T(8,128)(2,1)S(1)}, u32[]{:S(2)}, u32[]{:S(2)}) %all-to-all-start.2) | async-done | bytes 3145760 | tf_op jit(solution)/shard_map/all_to_all | solution.py:80
  100.0 4.3 %all-to-all-start = ((bf16[4,128,512]{2,1,0:T(8,128)(2,1)}), bf16[4,128,512]{2,1,0:T(8,128)(2,1)}, u32[]{:S(2)}, u32[]{:S(2)}) async-start(bf16[4,128,512]{2,1,0:T(8,128)(2,1)} %pad_maximum_fusion.1), calls=%async_computation | async-start | bytes 1048576 | tf_op jit(solution)/shard_map/all_to_all | solution.py:108
  104.3 2.5 %gather_fusion.1 = bf16[48,64,512]{2,1,0:T(8,128)(2,1)} fusion(bf16[48,64,512]{2,1,0:T(8,128)(2,1)S(1)} %bitcast.79, s32[1024]{0:T(1024)S(1)} %pad_clamp_fusion), kind=kCustom, calls=%fused_computation.1 | custom fusion | bytes 6291648 | tf_op jit(solution)/shard_map/gather | solution.py:81
  106.8 2.1 %fusion.52 = (bf16[48,64,256]{2,1,0:T(8,128)(2,1)S(1)}, bf16[48,64,256]{2,1,0:T(8,128)(2,1)S(1)}) fusion(bf16[48,64,512]{2,1,0:T(8,128)(2,1)} %gather_fusion.1), kind=kLoop, calls=%fused_computation.107 | loop fusion | bytes 6291456 | tf_op jit(solution)/shard_map/slice | solution.py:83
  108.9 1.8 copy.43
  110.7 8.6 %fusion.8 = f32[3584,512,2]{1,0,2:T(8,128)} fusion(bf16[512,256]{1,0:T(8,128)(2,1)} %get-tuple-element.21, bf16[3072,256]{1,0:T(8,128)(2,1)S(1)} %bitcast.81, bf16[64,2,8,256]{3,2,1,0:T(8,128)(2,1)} %bitcast.88), kind=kOutput, calls=%fused_computation.18 | convolution fusion | flops 1882718208 | bytes 17039360 | tf_op jit(solution)/shard_map/rhd,kd->hrk/dot_general | solution.py:92
  119.3 16.0 %fusion.53 = (f32[2,512]{1,0:T(2,128)S(1)}, f32[2,512,3584]{1,2,0:T(8,128)}) fusion(f32[3584,512,2]{1,0,2:T(8,128)} %fusion.8, pred[512,3584]{0,1:T(8,128)(4,1)S(1)} %copy-done), kind=kOutput, calls=%fused_computation.108 | output fusion | flops 22023680 | bytes 31199232 | tf_op jit(solution)/shard_map/sub | solution.py:97
  135.3 7.3 %fusion.12 = bf16[512,2,256]{0,2,1:T(8,128)(2,1)S(1)} fusion(f32[2,512,3584]{1,2,0:T(8,128)} %get-tuple-element.16, f32[2,512]{1,0:T(2,128)S(1)} %get-tuple-element.15, bf16[512,256]{0,1:T(8,128)(2,1)} %copy.51, bf16[3072,256]{0,1:T(8,128)(2,1)S(1)} %copy-done.1), kind=kOutput, calls=%fused_computation.22 | convolution fusion | flops 1890320384 | bytes 17043456 | tf_op jit(solution)/shard_map/hrk,kd->rhd/dot_general | solution.py:99
  142.8 0.9 copy.46
  143.6 3.5 %all-to-all-start.3 = ((bf16[4,128,512]{1,2,0:T(8,128)(2,1)}), bf16[4,128,512]{1,2,0:T(8,128)(2,1)S(1)}, u32[]{:S(2)}, u32[]{:S(2)}) async-start(bf16[4,128,512]{1,2,0:T(8,128)(2,1)} %copy.46), calls=%async_computation.3 | async-start | bytes 1048576 | tf_op jit(solution)/shard_map/all_to_all | solution.py:111
  147.2 0.7 all-gather.8.cloned.1.call-update
  147.9 9.0 %all-gather = bf16[4,1,512]{2,1,0:T(2,128)(2,1)S(1)} all-gather(bf16[1,1,512]{2,1,0:T(2,128)(2,1)S(1)} %reshape.209), channel_id=1, replica_groups=mesh['req'=8,'tp'=4] {'tp'}, dimensions={0}, use_global_device_ids=true | all-gather | bytes 5120 | tf_op jit(solution)/shard_map/all_gather | solution.py:105
  156.9 5.2 %all-gather.1 = bf16[4,1,512]{2,1,0:T(2,128)(2,1)S(1)} all-gather(bf16[1,1,512]{2,1,0:T(2,128)(2,1)S(1)} %reshape.211), channel_id=1, replica_groups=mesh['req'=8,'tp'=4] {'tp'}, dimensions={0}, use_global_device_ids=true | all-gather | bytes 5120 | tf_op jit(solution)/shard_map/all_gather | solution.py:106
  162.1 1.2 convert_bitcast_fusion
  163.4 4.8 %multiply_reduce_fusion.1 = (f32[128]{0:T(128)S(1)}, f32[128,2048]{1,0:T(8,128)S(1)}) fusion(bf16[128,2048]{0,1:T(8,128)(2,1)S(1)} %bitcast.84, bf16[2048,2048]{1,0:T(8,128)(2,1)} %all-gather.6.cloned.1.call-done), kind=kOutput, calls=%fused_computation.27 | convolution fusion | flops 1074265984 | bytes 9961984 | tf_op jit(solution)/shard_map/dot_general | solution.py:114
  168.5 2.5 %multiply_reduce_fusion = (f32[128]{0:T(128)S(1)}, f32[128,2048]{1,0:T(8,128)S(1)}) fusion(bf16[256,2048]{1,0:T(8,128)(2,1)} %all-gather.10.cloned.1.call-done, bf16[512,256]{1,0:T(8,128)(2,1)} %param.25, s32[]{:T(128)S(6)} %select_n.68, bf16[128,2048]{1,0:T(8,128)(2,1)S(1)} %add_convert_fusion.1, bf16[2048,256]{1,0:T(8,128)(2,1)} %all-gather.8.cloned.1.call-done), kind=kOutput, calls=%fused_computation.25 | convolution fusion | flops 269320064 | bytes 3736068 | tf_op jit(solution)/shard_map/dot_general | solution.py:126
  171.2 11.2 %all_to_all.54 = bf16[128,4,512]{2,0,1:T(8,128)(2,1)S(1)} all-to-all(bf16[128,4,512]{2,0,1:T(8,128)(2,1)S(1)} %bitcast.86), channel_id=1, replica_groups=mesh['req'=8,'tp'=4] {'tp'}, dimensions={1} | all-to-all | bytes 1048576 | tf_op jit(solution)/shard_map/all_to_all | solution.py:134
  182.5 0.8 copy.62
  (59 shorter events, 4.4 us)
Async XLA Ops:
  6.5 156.9 %all-gather.6.cloned.1.call-start = ((), (), s32[]{:S(2)}) async-start(), calls=%async_computation.5 | async-start | bytes 10485760 | tf_op jit(solution)/shard_map/all_gather | solution.py:102
  10.4 13.7 %all-to-all-start.1 = ((s32[8,1,6]{2,1,0:T(1,128)}), s32[8,1,6]{2,1,0:T(1,128)S(1)}, u32[]{:S(2)}, u32[]{:S(2)}) async-start(s32[8,1,6]{2,1,0:T(1,128)} %copy.41), calls=%async_computation.1 | async-start | bytes 8192 | tf_op jit(solution)/shard_map/all_to_all | solution.py:73
  26.7 4.6 %copy-start.5 = (s32[1,8]{1,0:T(1,128)S(1)}, s32[1,8]{1,0:T(1,128)}, u32[]{:S(2)}) copy-start(s32[1,8]{1,0:T(1,128)} %param.31) | copy-start | bytes 100
  26.7 4.8 %copy-start.7 = (s32[1,8]{1,0:T(1,128)S(1)}, s32[1,8]{1,0:T(1,128)}, u32[]{:S(2)}) copy-start(s32[1,8]{1,0:T(1,128)} %param.33) | copy-start | bytes 100
  26.7 7.5 %copy-start.6 = (s32[48,1]{0,1:T(1,128)S(1)}, s32[48,1]{0,1:T(1,128)}, u32[]{:S(2)}) copy-start(s32[48,1]{0,1:T(1,128)} %param.29) | copy-start | bytes 580
  26.7 7.7 %copy-start.4 = (s32[1,8]{1,0:T(1,128)S(1)}, s32[1,8]{1,0:T(1,128)}, u32[]{:S(2)}) copy-start(s32[1,8]{1,0:T(1,128)} %param.32) | copy-start | bytes 100
  26.7 73.3 %all-to-all-start.2 = ((bf16[8,6,64,512]{3,2,1,0:T(8,128)(2,1)}), bf16[8,6,64,512]{3,2,1,0:T(8,128)(2,1)S(1)}, u32[]{:S(2)}, u32[]{:S(2)}) async-start(bf16[8,6,64,512]{3,2,1,0:T(8,128)(2,1)} %bitcast.80), calls=%async_computation.2 | async-start | bytes 6291456 | tf_op jit(solution)/shard_map/all_to_all | solution.py:80
  30.5 138.0 %all-gather.10.cloned.1.call-start = ((), (), s32[]{:S(2)}) async-start(), calls=%async_computation.7 | async-start | bytes 1310720 | tf_op jit(solution)/shard_map/all_gather | solution.py:104
  100.0 43.7 %all-to-all-start = ((bf16[4,128,512]{2,1,0:T(8,128)(2,1)}), bf16[4,128,512]{2,1,0:T(8,128)(2,1)}, u32[]{:S(2)}, u32[]{:S(2)}) async-start(bf16[4,128,512]{2,1,0:T(8,128)(2,1)} %pad_maximum_fusion.1), calls=%async_computation | async-start | bytes 1048576 | tf_op jit(solution)/shard_map/all_to_all | solution.py:108
  110.7 8.6 %copy-start = (pred[512,3584]{0,1:T(8,128)(4,1)S(1)}, pred[512,3584]{0,1:T(8,128)(4,1)}, u32[]{:S(2)}) copy-start(pred[512,3584]{0,1:T(8,128)(4,1)} %pad_add_fusion) | copy-start | bytes 5505028
  119.3 16.0 %copy-start.1 = (bf16[3072,256]{0,1:T(8,128)(2,1)S(1)}, bf16[3072,256]{0,1:T(8,128)(2,1)}, u32[]{:S(2)}) copy-start(bf16[3072,256]{0,1:T(8,128)(2,1)} %copy.43) | copy-start | bytes 4718596
  142.6 5.2 %copy-start.2 = (bf16[512]{0:T(512)(128)(2,1)S(1)}, bf16[512]{0:T(512)(128)(2,1)}, u32[]{:S(2)}) copy-start(bf16[512]{0:T(512)(128)(2,1)} %param.24) | copy-start | bytes 3076
  142.6 14.3 %copy-start.3 = (bf16[512]{0:T(512)(128)(2,1)S(1)}, bf16[512]{0:T(512)(128)(2,1)}, u32[]{:S(2)}) copy-start(bf16[512]{0:T(512)(128)(2,1)} %param.28) | copy-start | bytes 3076
  143.6 19.7 %all-to-all-start.3 = ((bf16[4,128,512]{1,2,0:T(8,128)(2,1)}), bf16[4,128,512]{1,2,0:T(8,128)(2,1)S(1)}, u32[]{:S(2)}, u32[]{:S(2)}) async-start(bf16[4,128,512]{1,2,0:T(8,128)(2,1)} %copy.46), calls=%async_computation.3 | async-start | bytes 1048576 | tf_op jit(solution)/shard_map/all_to_all | solution.py:111
  147.1 21.4 %all-gather.8.cloned.1.call-start = ((), (), s32[]{:S(2)}) async-start(), calls=%async_computation.6 | async-start | bytes 1310720 | tf_op jit(solution)/shard_map/all_gather | solution.py:103
Sparse Core Ops, SparseCore 0:
  8.9 60.9 all-gather.5
  71.5 16.7 all-gather.9
  149.5 16.2 all-gather.7
